TPU v7x, 128 devices: a whole 4x4x4 slice. The times are simulated.
128 devices in a mesh: mode: 8 (over x, core), member: 16 (over z, y).
Axes of the slice: x: 4, y: 4, z: 4, core: 2. Of those that a mesh axis runs over, the one named last changes fastest.
Arguments:
- ground_accel: bfloat16 [4, 639], replicated, may hold values from -6 to 6
- modal_kernel: bfloat16 [4096, 512], P(('mode', 'member')), may hold values from -0.25 to 0.25
- mode_shapes: bfloat16 [98304, 4096], P('member', 'mode'), may hold values from -0.09375 to 0.09375
- member_owner: int32 [16384, 1], P('member'), may hold values from 0 to 127; in each aligned block of 128 rows (0 to 127, 128 to 255, ...) at most 2 rows name the same one
- member_group: int32 [16384, 1], P('member'), may hold values from 0 to 3
- record_table: int32 [512, 8], P(('mode', 'member')), may hold values from 0 to 3
- case_coef: float32 [8, 6], replicated, may hold values from -1.5 to 1.5
- gravity: float32 [512, 8], P(('mode', 'member')), may hold values from -10 to 10
Outputs:
- demand: float32 [512, 8], P(('mode', 'member'))
Inputs may be any that keep to these rules, and one draw needn't show every extreme that they name: `member_owner`: in each aligned block of 1024 / 8 members no owner is named more than 2 times, a bound that some block reaches.
All inputs are finite; a program needn't handle non-finite values.
Results may differ from a plain program's by a relative error of at most 0.0065.
Values may be sent and summed in bfloat16 or wider, within the bound.
No kernel may reach another device: no remote copies, remote signals or barrier semaphores. Data moves between devices by JAX's collectives and lax.ppermute only.
A program may use at most 64 MiB of HBM per device.

v0:
```python
import jax
import jax.numpy as jnp
from jax import lax
from jax.sharding import PartitionSpec as P


def lagged_table(ground_accel, tap_count):
    record_count, span_len = ground_accel.shape
    step_count = span_len - tap_count + 1
    tiled = jnp.tile(ground_accel, (1, step_count + 1))[:, : step_count * (span_len + 1)]
    windows = tiled.reshape(record_count, step_count, span_len + 1)[:, :, :tap_count]
    return windows.reshape(record_count * step_count, tap_count)


def local(
    ground_accel,
    modal_kernel,
    mode_shapes,
    member_owner,
    member_group,
    record_table,
    case_coef,
    gravity,
):
    tap_count = modal_kernel.shape[1]
    record_count = ground_accel.shape[0]
    comp_count = case_coef.shape[1]
    n_mode = lax.axis_size("mode")
    n_member = lax.axis_size("member")
    groups_here = gravity.shape[0]
    group_total = groups_here * n_mode * n_member
    lagged = lagged_table(ground_accel, tap_count)
    local_resp = lax.dot_general(
        modal_kernel[:, ::-1], lagged, (((1,), (1,)), ((), ())), preferred_element_type=jnp.float32
    ).astype(jnp.bfloat16)
    modal_resp = lax.all_gather(local_resp, "member", axis=0, tiled=True)
    partial = jnp.dot(mode_shapes, modal_resp, preferred_element_type=jnp.float32).astype(
        jnp.bfloat16
    )
    members_here = member_owner.shape[0]
    packed = partial.reshape(members_here, comp_count * partial.shape[1])
    group_index = member_owner[:, 0] * groups_here + member_group[:, 0]
    selector = (jnp.arange(group_total)[:, None] == group_index[None, :]).astype(jnp.bfloat16)
    group_part = jnp.dot(selector, packed, preferred_element_type=jnp.float32)
    by_mode = lax.psum_scatter(
        group_part.astype(jnp.bfloat16), "mode", scatter_dimension=0, tiled=True
    )
    group_sums = lax.psum_scatter(
        by_mode.astype(jnp.float32), "member", scatter_dimension=0, tiled=True
    )
    group_sums = group_sums.reshape(groups_here, comp_count, record_count, -1)
    case_mix = jnp.einsum("sc,gcrt->gsrt", case_coef, group_sums, precision=lax.Precision.HIGHEST)
    record_pick = (record_table[:, :, None] == jnp.arange(record_count)[None, None, :]).astype(
        jnp.float32
    )
    selected = jnp.sum(record_pick[:, :, :, None] * case_mix, axis=2)
    combined = gravity[:, :, None] + selected
    return jnp.max(jnp.abs(combined), axis=2)


def solution(mesh):
    placed = (
        P(),
        P(("mode", "member"), None),
        P("member", "mode"),
        P("member", None),
        P("member", None),
        P(("mode", "member"), None),
        P(),
        P(("mode", "member"), None),
    )
    return jax.shard_map(
        local, mesh=mesh, in_specs=placed, out_specs=P(("mode", "member"), None), check_vma=False
    )
```

profile of v0, /device:TPU:0, one launch (start us, length us, event | category | flops | bytes accessed | tf_op | source)
XLA Modules:
  0.0 198.6 jit_solution(844657869856164750)
XLA Ops:
  6.5 0.0 copy-start
  6.5 0.0 reduce-scatter.2.cloned.1.call-start
  6.5 0.8 tile.4
  7.3 0.6 tile.10
  7.9 0.2 slice.8
  8.2 0.1 copy.21
  8.3 1.6 rev.3
  9.9 0.2 convolution_convert_fusion.2
  10.2 25.6 %all_gather.3 = bf16[512,512]{1,0:T(8,128)(2,1)S(1)} all-gather(bf16[32,512]{1,0:T(8,128)(2,1)S(1)} %convolution_convert_fusion.2), channel_id=1, replica_groups=mesh['mode'=8,'member'=16] {'member'}, dimensions={0}, use_global_device_ids=true | all-gather | bytes 557056 | tf_op jit(solution)/shard_map/all_gather | solution.py:36
  35.8 8.2 %fusion = bf16[6144,512]{0,1:T(8,128)(2,1)} fusion(bf16[512,512]{1,0:T(8,128)(2,1)S(1)} %all_gather.3, bf16[6144,512]{1,0:T(8,128)(2,1)} %param.10), kind=kOutput, calls=%fused_computation.1 | convolution fusion | flops 3224371200 | bytes 13107200 | tf_op jit(solution)/shard_map/dot_general | solution.py:37
  44.0 8.7 %copy.14 = bf16[6144,512]{1,0:T(8,128)(2,1)} copy(bf16[6144,512]{0,1:T(8,128)(2,1)} %fusion) | data formatting | bytes 12582912 | tf_op jit(solution)/shard_map/convert_element_type | solution.py:37
  52.7 11.5 %reshape.37 = bf16[1024,3072]{1,0:T(8,128)(2,1)} reshape(bf16[6144,512]{1,0:T(8,128)(2,1)} %copy.14) | data formatting | bytes 12582912 | tf_op jit(solution)/shard_map/reshape | solution.py:41
  64.2 0.0 copy-done.2
  64.2 0.0 copy-start.5
  64.2 0.0 copy-start.3
  64.2 0.0 copy-start.4
  64.3 7.6 %convolution_convert_fusion.1 = bf16[512,3072]{1,0:T(8,128)(2,1)} fusion(bf16[1024,3072]{1,0:T(8,128)(2,1)} %reshape.37, s32[1024]{0:T(1024)S(1)} %bitcast.28), kind=kOutput, calls=%fused_computation.2 | convolution fusion | flops 3223322624 | bytes 9441280 | tf_op jit(solution)/shard_map/dot_general | solution.py:44
  71.8 0.0 reduce-scatter.2.cloned.1.call-update
  71.8 0.0 copy-done.5
  71.9 0.6 dynamic-slice
  73.1 33.8 %reduce-scatter.2.cloned.1.call-done = bf16[64,3072]{1,0:T(8,128)(2,1)} async-done(((bf16[512,3072]{1,0:T(8,128)(2,1)}), bf16[64,3072]{1,0:T(8,128)(2,1)}) %reduce-scatter.2.cloned.1.call-update) | async-done | bytes 393232 | tf_op jit(solution)/shard_map/reduce_scatter | solution.py:45
  107.0 83.7 %all-reduce.2 = f32[64,3072]{1,0:T(8,128)S(1)} all-reduce(bf16[64,3072]{1,0:T(8,128)(2,1)} %reduce-scatter.2.cloned.1.call-done), channel_id=3, replica_groups=mesh['mode'=8,'member'=16] {'member'}, use_global_device_ids=true, to_apply=%region_1.0.clone | all-reduce | flops 196608 | bytes 1179648
  190.8 0.2 fusion.2
  191.0 0.7 abs_reduce_fusion
  (11 shorter events, 0.1 us)
Async XLA Ops:
  6.5 184.2 %copy-start = (f32[8,6]{1,0:T(8,128)S(1)}, f32[8,6]{1,0:T(8,128)}, u32[]{:S(2)}) copy-start(f32[8,6]{1,0:T(8,128)} %param.14) | copy-start | bytes 580
  6.5 100.4 %reduce-scatter.2.cloned.1.call-start = ((), (), s32[]{:S(2)}) async-start(), calls=%async_computation.1 | async-start | bytes 3538944 | tf_op jit(solution)/shard_map/reduce_scatter | solution.py:45
  52.7 11.5 %copy-start.1 = (s32[1024,1]{0,1:T(1,128)S(1)}, s32[1024,1]{0,1:T(1,128)}, u32[]{:S(2)}) copy-start(s32[1024,1]{0,1:T(1,128)} %param.12) | copy-start | bytes 12292
  52.7 11.5 %copy-start.2 = (s32[1024,1]{0,1:T(1,128)S(1)}, s32[1024,1]{0,1:T(1,128)}, u32[]{:S(2)}) copy-start(s32[1024,1]{0,1:T(1,128)} %param.11) | copy-start | bytes 12292
  64.2 7.6 %copy-start.5 = (u32[128]{0:T(128)S(1)}, u32[128]{0:T(128)}, u32[]{:S(2)}) copy-start(u32[128]{0:T(128)} %constant.11) | copy-start | bytes 1540
  64.2 8.9 %copy-start.3 = (s32[4,8]{1,0:T(4,128)S(1)}, s32[4,8]{1,0:T(4,128)}, u32[]{:S(2)}) copy-start(s32[4,8]{1,0:T(4,128)} %param.13) | copy-start | bytes 388
  64.2 126.7 %copy-start.4 = (f32[4,8]{1,0:T(4,128)S(1)}, f32[4,8]{1,0:T(4,128)}, u32[]{:S(2)}) copy-start(f32[4,8]{1,0:T(4,128)} %param.15) | copy-start | bytes 388
Sparse Core Ops, SparseCore 0:
  72.0 34.9 reduce-scatter.1
where the time goes:
time: 199 us
  blocking collectives  109 us (55%)
  waiting for transfers between devices  33.9 us (17%)
  local copies, waits for them, and re-layouts  24.2 us (12%)
  matrix products  16.2 us (8%)
  between operations  14.2 us (7%)
    unnamed x1, blocking collectives  83.7 us
    reduce_scatter x1, waiting for transfers between devices, local(): lax.psum_scatter(group_part.astype(jnp.bfloat16), 'mode', scatter_dimensi...  33.8 us
    all_gather x1, blocking collectives, local(): modal_resp = lax.all_gather(local_resp, 'member', axis=0, tiled=True)  25.6 us
    reshape x1, local copies, waits for them, and re-layouts, local(): packed = partial.reshape(members_here, comp_count * partial.shape[1])  11.5 us
    convert_element_type x1, local copies, waits for them, and re-layouts, local(): jnp.dot(mode_shapes, modal_resp, preferred_element_type=jnp.float32)  8.68 us
    dot_general x1, matrix products, local(): jnp.dot(mode_shapes, modal_resp, preferred_element_type=jnp.float32)  8.21 us
    dot_general x1, matrix products, local(): group_part = jnp.dot(selector, packed, preferred_element_type=jnp.float32)  7.56 us
  transfers between devices with their start and end apart: 1, of which 1 were waited for; matrix products, arithmetic and copies ran while one was open for 0% of the time, Pallas kernels for 0%

commit v1 on v0

--- a/solution.py
+++ b/solution.py
@@ -33,7 +33,8 @@
     local_resp = lax.dot_general(
         modal_kernel[:, ::-1], lagged, (((1,), (1,)), ((), ())), preferred_element_type=jnp.float32
     ).astype(jnp.bfloat16)
-    modal_resp = lax.all_gather(local_resp, "member", axis=0, tiled=True)
+    opened = jnp.concatenate(lax.axis_size("member") * [local_resp], axis=0)
+    modal_resp = lax.all_to_all(opened, "member", 0, 0, tiled=True)
     partial = jnp.dot(mode_shapes, modal_resp, preferred_element_type=jnp.float32).astype(
         jnp.bfloat16
     )

time: 199 us -> 201 us (1.010)
  blocking collectives: 109 us -> 83.7 us
  waiting for transfers between devices: 33.9 us -> 43.5 us
  local copies, waits for them, and re-layouts: 24.2 us -> 33.4 us
  starting transfers between devices: 0.01 us -> 8.17 us
    all_gather x1 -> x0, blocking collectives: 25.6 us -> none  [local(): modal_resp = lax.all_gather(local_resp, 'member', axis=0, tiled=True)]
    all_to_all x0 -> x1, waiting for transfers between devices: none -> 11.4 us  [local(): modal_resp = lax.all_to_all(opened, 'member', 0, 0, tiled=True)]
    unnamed x15 -> x29, local copies, waits for them, and re-layouts: 0.71 us -> 9.28 us
    all_to_all x0 -> x1, starting transfers between devices: none -> 8.13 us  [local(): modal_resp = lax.all_to_all(opened, 'member', 0, 0, tiled=True)]
  transfers between devices with their start and end apart: 1 -> 2, of which waited for: 1 -> 2; matrix products, arithmetic and copies ran while one was open for 0% -> 0% of each run, Pallas kernels for 0% -> 0%
where the time goes in v1:
time: 201 us
  blocking collectives  83.7 us (42%)
  waiting for transfers between devices  43.5 us (22%)
  local copies, waits for them, and re-layouts  33.4 us (17%)
  matrix products  16.9 us (8%)
  between operations  14.2 us (7%)
  starting transfers between devices  8.17 us (4%)
    unnamed x1, blocking collectives  83.7 us
    reduce_scatter x1, waiting for transfers between devices, local(): lax.psum_scatter(group_part.astype(jnp.bfloat16), 'mode', scatter_dimensi...  32 us
    reshape x1, local copies, waits for them, and re-layouts, local(): packed = partial.reshape(members_here, comp_count * partial.shape[1])  11.5 us
    all_to_all x1, waiting for transfers between devices, local(): modal_resp = lax.all_to_all(opened, 'member', 0, 0, tiled=True)  11.4 us
    unnamed x29, local copies, waits for them, and re-layouts  9.28 us
    convert_element_type x1, local copies, waits for them, and re-layouts, local(): jnp.dot(mode_shapes, modal_resp, preferred_element_type=jnp.float32)  8.68 us
    dot_general x1, matrix products, local(): jnp.dot(mode_shapes, modal_resp, preferred_element_type=jnp.float32)  8.2 us
    all_to_all x1, starting transfers between devices, local(): modal_resp = lax.all_to_all(opened, 'member', 0, 0, tiled=True)  8.13 us
  transfers between devices with their start and end apart: 2, of which 2 were waited for; matrix products, arithmetic and copies ran while one was open for 0% of the time, Pallas kernels for 0%

profile of v1, /device:TPU:0, one launch (start us, length us, event | category | flops | bytes accessed | tf_op | source)
XLA Modules:
  0.0 200.6 jit_solution(6733868398140942775)
XLA Ops:
  6.5 0.8 tile.4
  7.3 0.6 tile.10
  8.3 1.6 rev.3
  10.0 0.9 constant_dynamic-update-slice_fusion.15
  10.9 0.6 constant_dynamic-update-slice_fusion.14
  11.5 0.6 constant_dynamic-update-slice_fusion.13
  12.1 0.6 constant_dynamic-update-slice_fusion.12
  13.3 0.6 constant_dynamic-update-slice_fusion.10
  13.9 0.6 constant_dynamic-update-slice_fusion.9
  14.5 0.6 constant_dynamic-update-slice_fusion.8
  15.2 0.6 constant_dynamic-update-slice_fusion.7
  15.8 0.6 constant_dynamic-update-slice_fusion.6
  16.4 0.6 constant_dynamic-update-slice_fusion.5
  17.6 0.6 constant_dynamic-update-slice_fusion.3
  18.2 0.6 constant_dynamic-update-slice_fusion.2
  20.1 8.1 %all-to-all-start = ((bf16[16,32,512]{2,1,0:T(8,128)(2,1)}), bf16[16,32,512]{2,1,0:T(8,128)(2,1)S(1)}, u32[]{:S(2)}, u32[]{:S(2)}) async-start(bf16[16,32,512]{2,1,0:T(8,128)(2,1)} %bitcast.2), calls=%async_computation | async-start | bytes 1048576 | tf_op jit(solution)/shard_map/all_to_all | solution.py:37
  28.3 11.4 %all-to-all-done = bf16[16,32,512]{2,1,0:T(8,128)(2,1)S(1)} async-done(((bf16[16,32,512]{2,1,0:T(8,128)(2,1)}), bf16[16,32,512]{2,1,0:T(8,128)(2,1)S(1)}, u32[]{:S(2)}, u32[]{:S(2)}) %all-to-all-start) | async-done | bytes 524320 | tf_op jit(solution)/shard_map/all_to_all | solution.py:37
  39.7 8.2 %fusion = bf16[6144,512]{0,1:T(8,128)(2,1)} fusion(bf16[512,512]{1,0:T(8,128)(2,1)S(1)} %bitcast.30, bf16[6144,512]{1,0:T(8,128)(2,1)} %param.10), kind=kOutput, calls=%fused_computation.1 | convolution fusion | flops 3224371200 | bytes 13107200 | tf_op jit(solution)/shard_map/dot_general | solution.py:38
  47.9 8.7 %copy.14 = bf16[6144,512]{1,0:T(8,128)(2,1)} copy(bf16[6144,512]{0,1:T(8,128)(2,1)} %fusion) | data formatting | bytes 12582912 | tf_op jit(solution)/shard_map/convert_element_type | solution.py:38
  56.6 11.5 %reshape.39 = bf16[1024,3072]{1,0:T(8,128)(2,1)} reshape(bf16[6144,512]{1,0:T(8,128)(2,1)} %copy.14) | data formatting | bytes 12582912 | tf_op jit(solution)/shard_map/reshape | solution.py:42
  68.1 7.6 %convolution_convert_fusion.1 = bf16[512,3072]{1,0:T(8,128)(2,1)} fusion(bf16[1024,3072]{1,0:T(8,128)(2,1)} %reshape.39, s32[1024]{0:T(1024)S(1)} %bitcast.31), kind=kOutput, calls=%fused_computation.2 | convolution fusion | flops 3223322624 | bytes 9441280 | tf_op jit(solution)/shard_map/dot_general | solution.py:45
  77.0 32.0 %reduce-scatter.2.cloned.1.call-done = bf16[64,3072]{1,0:T(8,128)(2,1)} async-done(((bf16[512,3072]{1,0:T(8,128)(2,1)}), bf16[64,3072]{1,0:T(8,128)(2,1)}) %reduce-scatter.2.cloned.1.call-update) | async-done | bytes 393232 | tf_op jit(solution)/shard_map/reduce_scatter | solution.py:46
  109.0 83.7 %all-reduce.2 = f32[64,3072]{1,0:T(8,128)S(1)} all-reduce(bf16[64,3072]{1,0:T(8,128)(2,1)} %reduce-scatter.2.cloned.1.call-done), channel_id=3, replica_groups=mesh['mode'=8,'member'=16] {'member'}, use_global_device_ids=true, to_apply=%region_1.0.clone | all-reduce | flops 196608 | bytes 1179648
  193.0 0.7 abs_reduce_fusion
  (27 shorter events, 3.7 us)
Async XLA Ops:
  6.5 186.3 %copy-start = (f32[8,6]{1,0:T(8,128)S(1)}, f32[8,6]{1,0:T(8,128)}, u32[]{:S(2)}) copy-start(f32[8,6]{1,0:T(8,128)} %param.14) | copy-start | bytes 580
  6.5 21.7 %copy-start.2 = (s32[1024,1]{0,1:T(1,128)S(1)}, s32[1024,1]{0,1:T(1,128)}, u32[]{:S(2)}) copy-start(s32[1024,1]{0,1:T(1,128)} %param.11) | copy-start | bytes 12292
  6.5 21.7 %copy-start.1 = (s32[1024,1]{0,1:T(1,128)S(1)}, s32[1024,1]{0,1:T(1,128)}, u32[]{:S(2)}) copy-start(s32[1024,1]{0,1:T(1,128)} %param.12) | copy-start | bytes 12292
  20.1 19.7 %all-to-all-start = ((bf16[16,32,512]{2,1,0:T(8,128)(2,1)}), bf16[16,32,512]{2,1,0:T(8,128)(2,1)S(1)}, u32[]{:S(2)}, u32[]{:S(2)}) async-start(bf16[16,32,512]{2,1,0:T(8,128)(2,1)} %bitcast.2), calls=%async_computation | async-start | bytes 1048576 | tf_op jit(solution)/shard_map/all_to_all | solution.py:37
  28.2 80.8 %reduce-scatter.2.cloned.1.call-start = ((), (), s32[]{:S(2)}) async-start(), calls=%async_computation.2 | async-start | bytes 3538944 | tf_op jit(solution)/shard_map/reduce_scatter | solution.py:46
  68.1 7.6 %copy-start.5 = (u32[128]{0:T(128)S(1)}, u32[128]{0:T(128)}, u32[]{:S(2)}) copy-start(u32[128]{0:T(128)} %constant.11) | copy-start | bytes 1540
  68.1 8.9 %copy-start.3 = (s32[4,8]{1,0:T(4,128)S(1)}, s32[4,8]{1,0:T(4,128)}, u32[]{:S(2)}) copy-start(s32[4,8]{1,0:T(4,128)} %param.13) | copy-start | bytes 388
  68.1 124.9 %copy-start.4 = (f32[4,8]{1,0:T(4,128)S(1)}, f32[4,8]{1,0:T(4,128)}, u32[]{:S(2)}) copy-start(f32[4,8]{1,0:T(4,128)} %param.15) | copy-start | bytes 388
Sparse Core Ops, SparseCore 0:
  75.8 33.1 reduce-scatter.1
